TPU v7x, 32 devices: a whole 2x2x4 slice. The times are simulated.
32 devices in a mesh: occ: 4 (over z), aux: 4 (over x, core), vir: 2 (over y).
Axes of the slice: x: 2, y: 2, z: 4, core: 2. Of those that a mesh axis runs over, the one named last changes fastest.
Arguments:
- integrals: bfloat16 [4, 2048, 4096], P('occ', 'vir', 'aux'), may hold values from -0.65625 to 0.65625
- occ_energy: float32 [4], replicated, may hold values from -2 to -0.5
- vir_energy: float32 [2048], replicated, may hold values from 0.25 to 3
Outputs:
- lagrangian: bfloat16 [4, 2048, 4096], P('occ', 'vir', 'aux')
All inputs are finite; a program needn't handle non-finite values.
Results may differ from a plain program's by a relative error of at most 0.0039.
Values may be sent and summed in bfloat16 or wider, within the bound.
No kernel may reach another device: no remote copies, remote signals or barrier semaphores. Data moves between devices by JAX's collectives and lax.ppermute only.
A program may use at most 64 MiB of HBM per device.

v0:
```python
import jax
import jax.numpy as jnp
from jax import lax
from jax.sharding import PartitionSpec as P

CHUNKS = 4
AUX_BY_PERMUTE = False
Z_GATED = False


def shifted_2(value, axis, by):
    count = lax.axis_size(axis)
    return lax.ppermute(value, axis, [(i, (i + by) % count) for i in range(count)])


def general_plan(integrals, occ_energy, vir_energy):
    row_count = integrals.shape[0]
    vir_width = integrals.shape[1]
    cycle_size = lax.axis_size("occ")
    position = lax.axis_index("occ")
    own_level = lax.dynamic_slice_in_dim(occ_energy, position * row_count, row_count)
    partner_level = lax.dynamic_slice_in_dim(
        occ_energy, (position - 2) % cycle_size * row_count, row_count
    )
    local_vir = lax.dynamic_slice_in_dim(vir_energy, lax.axis_index("vir") * vir_width, vir_width)
    shifted = shifted_2(integrals, "occ", 2)
    partner = lax.all_gather(shifted, "vir", axis=1, tiled=True)
    virtuals = partner.shape[1]
    pair_level = own_level + partner_level
    share_rows = virtuals // lax.axis_size("aux")
    partial_value = lax.psum_scatter(
        jnp.einsum("nbq,naq->bna", partner, integrals, preferred_element_type=jnp.float32),
        "aux",
        scatter_dimension=0,
        tiled=True,
    )
    first_row = lax.axis_index("aux") * share_rows
    vir_rows = lax.dynamic_slice_in_dim(vir_energy, first_row, share_rows)
    amplitudes = (
        partial_value
        / (pair_level[None, :, None] - vir_rows[:, None, None] - local_vir[None, None, :])
    ).astype(jnp.bfloat16)
    portion = lax.all_gather(amplitudes, "aux", axis=0, tiled=True)
    own_part = jnp.einsum("bna,nbq->naq", portion, partner, preferred_element_type=jnp.float32)
    rows_back = jnp.einsum("bna,naq->nbq", portion, integrals, preferred_element_type=jnp.float32)
    owned = lax.psum_scatter(rows_back, "vir", scatter_dimension=1, tiled=True)
    returned = shifted_2(owned, "occ", -2)
    return (own_part + returned).astype(jnp.bfloat16)


def xor_pairs(count, step):
    return [(j, j ^ step) for j in range(count)]


def aux_reduce_scatter(x):
    count = lax.axis_size("aux")
    k = lax.axis_index("aux")
    first = 0
    step = 1
    while step < count:
        half = x.shape[0] // 2
        bit = k // step % 2
        keep = lax.dynamic_slice_in_dim(x, bit * half, half, 0)
        send = lax.dynamic_slice_in_dim(x, (1 - bit) * half, half, 0)
        x = keep + lax.ppermute(send, "aux", xor_pairs(count, step))
        first = first + bit * half
        step *= 2
    return (x, first)


def aux_all_gather(x):
    count = lax.axis_size("aux")
    k = lax.axis_index("aux")
    step = count // 2
    while step >= 1:
        bit = k // step % 2
        other = lax.ppermute(x, "aux", xor_pairs(count, step))
        x = jnp.where(bit == 0, jnp.concatenate([x, other]), jnp.concatenate([other, x]))
        step //= 2
    return x


def paired_plan(integrals, occ_energy, vir_energy):
    own = integrals[0]
    vir_rows, _ = own.shape
    cycle_size = lax.axis_size("occ")
    position = lax.axis_index("occ")
    pair_level = occ_energy[position] + occ_energy[(position - 2) % cycle_size]
    vir_pos = lax.axis_index("vir")
    vir_count = lax.axis_size("vir")
    aux_count = lax.axis_size("aux")
    share = vir_rows // aux_count
    width = vir_rows // CHUNKS
    if not AUX_BY_PERMUTE:
        first_row = lax.axis_index("aux") * share

    def forward(c, arrived):
        if vir_count == 2:
            mate = shifted_2(arrived, "vir", 1)
            block = jnp.concatenate([arrived, mate])
            cols = [vir_pos, 1 - vir_pos]
        else:
            block = lax.all_gather(arrived, "vir", axis=0, tiled=True)
            cols = list(range(vir_count))
        col_level = jnp.concatenate(
            [lax.dynamic_slice_in_dim(vir_energy, w * vir_rows + c * width, width) for w in cols]
        )
        return (block, col_level)

    def reduce(block):
        partial = jnp.einsum("aq,bq->ab", own, block, preferred_element_type=jnp.float32)
        if AUX_BY_PERMUTE:
            return aux_reduce_scatter(partial)
        return (lax.psum_scatter(partial, "aux", scatter_dimension=0, tiled=True), first_row)

    def amplitudes_of(summed, first, col_level):
        row_level = lax.dynamic_slice_in_dim(vir_energy, vir_pos * vir_rows + first, share)
        amplitudes = (summed / (pair_level - row_level[:, None] - col_level[None, :])).astype(
            jnp.bfloat16
        )
        if AUX_BY_PERMUTE:
            return aux_all_gather(amplitudes)
        return lax.all_gather(amplitudes, "aux", axis=0, tiled=True)

    arrived = [None] * CHUNKS
    blocks = [None] * CHUNKS
    levels = [None] * CHUNKS
    summed = [None] * CHUNKS
    firsts = [None] * CHUNKS
    gathered = [None] * CHUNKS
    total = None
    for c in range(CHUNKS if not Z_GATED else 0):
        arrived[c] = shifted_2(own[c * width : (c + 1) * width], "occ", 2)
    for t in range(CHUNKS + 4):
        piece = own[t * width : (t + 1) * width] if Z_GATED and t < CHUNKS else None
        if t > 0:
            gate = {"arrived": arrived[t - 1] if t - 1 < CHUNKS else None}
            if piece is not None:
                gate["piece"] = piece
            if 0 <= t - 2 < CHUNKS:
                gate["block"] = blocks[t - 2]
            if 0 <= t - 3 < CHUNKS:
                gate["summed"] = summed[t - 3]
            if 0 <= t - 4 < CHUNKS:
                gate["gathered"] = gathered[t - 4]
            if total is not None:
                gate["total"] = total
            gate = lax.optimization_barrier(gate)
            if piece is not None:
                piece = gate["piece"]
            if t - 1 < CHUNKS:
                arrived[t - 1] = gate["arrived"]
            if 0 <= t - 2 < CHUNKS:
                blocks[t - 2] = gate["block"]
            if 0 <= t - 3 < CHUNKS:
                summed[t - 3] = gate["summed"]
            if 0 <= t - 4 < CHUNKS:
                gathered[t - 4] = gate["gathered"]
            if total is not None:
                total = gate["total"]
        if piece is not None:
            arrived[t] = shifted_2(piece, "occ", 2)
        c = t - 1
        if 0 <= c < CHUNKS:
            blocks[c], levels[c] = forward(c, arrived[c])
        c = t - 2
        if 0 <= c < CHUNKS:
            summed[c], firsts[c] = reduce(blocks[c])
        c = t - 3
        if 0 <= c < CHUNKS:
            gathered[c] = amplitudes_of(summed[c], firsts[c], levels[c])
        c = t - 4
        if 0 <= c < CHUNKS:
            term = jnp.dot(gathered[c], blocks[c], preferred_element_type=jnp.float32)
            total = term if total is None else total + term
    gamma_own = total
    gamma_back = total
    return (gamma_own + gamma_back).astype(jnp.bfloat16)[None]


def on_device(integrals, occ_energy, vir_energy):
    cycle_size = lax.axis_size("occ")
    if integrals.shape[0] == 1 and 4 % cycle_size == 0 and (integrals.shape[1] % (CHUNKS * 8) == 0):
        return paired_plan(integrals, occ_energy, vir_energy)
    return general_plan(integrals, occ_energy, vir_energy)


def solution(mesh):
    placed = (P("occ", "vir", "aux"), P(), P())
    return jax.shard_map(
        on_device, mesh=mesh, in_specs=placed, out_specs=P("occ", "vir", "aux"), check_vma=False
    )
```

profile of v0, /device:TPU:0, one launch (start us, length us, event | category | flops | bytes accessed | tf_op | source)
XLA Modules:
  0.0 284.6 jit_solution(10130402411361232367)
XLA Ops:
  6.5 2.7 slice_bitcast_fusion
  9.2 4.0 %collective-permute-start.3 = (bf16[256,1024]{1,0:T(8,128)(2,1)S(1)}, bf16[256,1024]{1,0:T(8,128)(2,1)S(1)}, u32[]{:S(2)}, u32[]{:S(2)}) collective-permute-start(bf16[256,1024]{1,0:T(8,128)(2,1)S(1)} %get-tuple-element.41), channel_id=1, source_target_pairs={{0,16},{8,24},{16,0},{24,8},{1,17},{9,25},{17,1},{25,9},{2,18},{10... | collective-permute-start | bytes 1572872 | tf_op jit(solution)/shard_map/ppermute | solution.py:13
  13.3 23.2 %collective-permute-done.3 = bf16[256,1024]{1,0:T(8,128)(2,1)S(1)} collective-permute-done((bf16[256,1024]{1,0:T(8,128)(2,1)S(1)}, bf16[256,1024]{1,0:T(8,128)(2,1)S(1)}, u32[]{:S(2)}, u32[]{:S(2)}) %collective-permute-start.3) | collective-permute-done | bytes 524320 | tf_op jit(solution)/shard_map/ppermute | solution.py:13
  38.0 11.5 %collective-permute-done.4 = bf16[256,1024]{1,0:T(8,128)(2,1)S(1)} collective-permute-done((bf16[256,1024]{1,0:T(8,128)(2,1)S(1)}, bf16[256,1024]{1,0:T(8,128)(2,1)S(1)}, u32[]{:S(2)}, u32[]{:S(2)}) %collective-permute-start.4) | collective-permute-done | bytes 524320 | tf_op jit(solution)/shard_map/ppermute | solution.py:13
  49.6 13.1 %collective-permute-done.2 = bf16[256,1024]{1,0:T(8,128)(2,1)S(1)} collective-permute-done((bf16[256,1024]{1,0:T(8,128)(2,1)S(1)}, bf16[256,1024]{1,0:T(8,128)(2,1)S(1)}, u32[]{:S(2)}, u32[]{:S(2)}) %collective-permute-start.2) | collective-permute-done | bytes 524320 | tf_op jit(solution)/shard_map/ppermute | solution.py:13
  62.7 2.6 fusion.8
  68.2 9.3 %collective-permute-done.5 = bf16[256,1024]{1,0:T(8,128)(2,1)} collective-permute-done((bf16[256,1024]{1,0:T(8,128)(2,1)S(1)}, bf16[256,1024]{1,0:T(8,128)(2,1)}, u32[]{:S(2)}, u32[]{:S(2)}) %collective-permute-start.5) | collective-permute-done | bytes 524320 | tf_op jit(solution)/shard_map/ppermute | solution.py:13
  78.5 11.8 %collective-permute-done.1 = bf16[256,1024]{1,0:T(8,128)(2,1)S(1)} collective-permute-done((bf16[256,1024]{1,0:T(8,128)(2,1)}, bf16[256,1024]{1,0:T(8,128)(2,1)S(1)}, u32[]{:S(2)}, u32[]{:S(2)}) %collective-permute-start.1) | collective-permute-done | bytes 524320 | tf_op jit(solution)/shard_map/ppermute | solution.py:13
  90.4 4.3 %reduce-scatter.5.cloned.1.call-done = f32[256,512]{0,1:T(8,128)} async-done(((f32[1024,512]{0,1:T(8,128)}), f32[256,512]{0,1:T(8,128)}) %reduce-scatter.5.cloned.1.call-update) | async-done | bytes 524304 | tf_op jit(solution)/shard_map/reduce_scatter | solution.py:114
  96.7 4.2 %fusion.11 = f32[1024,512]{0,1:T(8,128)} fusion(bf16[512,1024]{1,0:T(8,128)(2,1)S(1)} %pad_maximum_fusion.1, bf16[1,1024,1024]{2,1,0:T(8,128)(2,1)} %param.3), kind=kOutput, calls=%fused_computation.11 | convolution fusion | flops 1073741824 | bytes 5242880 | tf_op jit(solution)/shard_map/aq,bq->ab/dot_general | solution.py:111
  104.9 9.8 %collective-permute-done.6 = bf16[256,1024]{1,0:T(8,128)(2,1)S(1)} collective-permute-done((bf16[256,1024]{1,0:T(8,128)(2,1)S(1)}, bf16[256,1024]{1,0:T(8,128)(2,1)S(1)}, u32[]{:S(2)}, u32[]{:S(2)}) %collective-permute-start.6) | collective-permute-done | bytes 524320 | tf_op jit(solution)/shard_map/ppermute | solution.py:13
  115.8 12.5 %collective-permute-done = bf16[256,1024]{1,0:T(8,128)(2,1)} collective-permute-done((bf16[256,1024]{1,0:T(8,128)(2,1)}, bf16[256,1024]{1,0:T(8,128)(2,1)}, u32[]{:S(2)}, u32[]{:S(2)}) %collective-permute-start) | collective-permute-done | bytes 524320 | tf_op jit(solution)/shard_map/ppermute | solution.py:13
  128.4 19.4 %reduce-scatter.7.cloned.1.call-done = f32[256,512]{0,1:T(8,128)} async-done(((f32[1024,512]{0,1:T(8,128)}), f32[256,512]{0,1:T(8,128)}) %reduce-scatter.7.cloned.1.call-update) | async-done | bytes 524304 | tf_op jit(solution)/shard_map/reduce_scatter | solution.py:114
  149.8 4.2 %fusion.14 = f32[1024,512]{0,1:T(8,128)} fusion(bf16[512,1024]{1,0:T(8,128)(2,1)S(1)} %pad_maximum_fusion.2, bf16[1,1024,1024]{2,1,0:T(8,128)(2,1)} %param.3), kind=kOutput, calls=%fused_computation.12 | convolution fusion | flops 1073741824 | bytes 5242880 | tf_op jit(solution)/shard_map/aq,bq->ab/dot_general | solution.py:111
  155.6 4.5 %fusion.23 = f32[1024,1024]{1,0:T(8,128)} fusion(bf16[1024,512]{0,1:T(8,128)(2,1)} %all-gather.5.cloned.1.call-done, bf16[512,1024]{1,0:T(8,128)(2,1)S(1)} %pad_maximum_fusion), kind=kOutput, calls=%fused_computation.34 | convolution fusion | flops 1073741824 | bytes 6291456 | tf_op jit(solution)/shard_map/dot_general | solution.py:174
  160.1 7.9 %collective-permute-done.7 = bf16[256,1024]{1,0:T(8,128)(2,1)S(1)} collective-permute-done((bf16[256,1024]{1,0:T(8,128)(2,1)}, bf16[256,1024]{1,0:T(8,128)(2,1)S(1)}, u32[]{:S(2)}, u32[]{:S(2)}) %collective-permute-start.7) | collective-permute-done | bytes 524320 | tf_op jit(solution)/shard_map/ppermute | solution.py:13
  169.1 31.4 %reduce-scatter.9.cloned.1.call-done = f32[256,512]{0,1:T(8,128)} async-done(((f32[1024,512]{0,1:T(8,128)}), f32[256,512]{0,1:T(8,128)}) %reduce-scatter.9.cloned.1.call-update) | async-done | bytes 524304 | tf_op jit(solution)/shard_map/reduce_scatter | solution.py:114
  202.6 4.2 %fusion.17 = f32[1024,512]{0,1:T(8,128)} fusion(bf16[512,1024]{1,0:T(8,128)(2,1)S(1)} %pad_maximum_fusion.3, bf16[1,1024,1024]{2,1,0:T(8,128)(2,1)} %param.3), kind=kOutput, calls=%fused_computation.13 | convolution fusion | flops 1073741824 | bytes 5242880 | tf_op jit(solution)/shard_map/aq,bq->ab/dot_general | solution.py:111
  210.3 2.9 %add.120 = f32[1024,1024]{1,0:T(8,128)} add(f32[1024,1024]{1,0:T(8,128)S(1)} %copy-done, f32[1024,1024]{1,0:T(8,128)S(1)} %fusion.24) | non-fusion elementwise | flops 1048576 | bytes 12582912 | tf_op jit(solution)/shard_map/add | solution.py:175
  213.2 6.3 %all-gather.9.cloned.1.call-done = bf16[1024,512]{0,1:T(8,128)(2,1)} async-done(((bf16[256,512]{0,1:T(8,128)(2,1)}), bf16[1024,512]{0,1:T(8,128)(2,1)}) %all-gather.9.cloned.1.call-update) | async-done | bytes 1048592 | tf_op jit(solution)/shard_map/all_gather | solution.py:123
  219.5 34.1 %reduce-scatter.11.cloned.1.call-done = f32[256,512]{0,1:T(8,128)} async-done(((f32[1024,512]{0,1:T(8,128)}), f32[256,512]{0,1:T(8,128)}) %reduce-scatter.11.cloned.1.call-update) | async-done | bytes 524304 | tf_op jit(solution)/shard_map/reduce_scatter | solution.py:114
  255.6 5.5 %convolution_add_fusion = f32[1024,1024]{1,0:T(8,128)} fusion(f32[1024,1024]{1,0:T(8,128)} %add.120, bf16[1024,512]{0,1:T(8,128)(2,1)S(1)} %copy-done.1, bf16[512,1024]{1,0:T(8,128)(2,1)S(1)} %pad_maximum_fusion.2), kind=kOutput, calls=%fused_computation.1 | convolution fusion | flops 1074790400 | bytes 10485760 | tf_op jit(solution)/shard_map/dot_general | solution.py:174
  261.1 11.5 %all-gather.11.cloned.1.call-done = bf16[1024,512]{0,1:T(8,128)(2,1)} async-done(((bf16[256,512]{0,1:T(8,128)(2,1)}), bf16[1024,512]{0,1:T(8,128)(2,1)}) %all-gather.11.cloned.1.call-update) | async-done | bytes 1048592 | tf_op jit(solution)/shard_map/all_gather | solution.py:123
  272.6 5.1 %fusion.20 = bf16[1,1024,1024]{2,1,0:T(8,128)(2,1)} fusion(f32[1024,1024]{1,0:T(8,128)} %convolution_add_fusion, bf16[1024,512]{0,1:T(8,128)(2,1)} %all-gather.11.cloned.1.call-done, bf16[512,1024]{1,0:T(8,128)(2,1)S(1)} %copy-done.5), kind=kOutput, calls=%fused_computation.14 | convolution fusion | flops 1076887552 | bytes 8388608 | tf_op jit(solution)/shard_map/dot_general | solution.py:174
  (58 shorter events, 23.6 us)
Async XLA Ops:
  6.5 88.2 %reduce-scatter.5.cloned.1.call-start = ((), (), s32[]{:S(2)}) async-start(), calls=%async_computation.4 | async-start | bytes 2621440 | tf_op jit(solution)/shard_map/reduce_scatter | solution.py:114
  9.2 53.4 %copy-start.2 = (bf16[1,1024,1024]{2,1,0:T(8,128)(2,1)S(1)}, bf16[1,1024,1024]{2,1,0:T(8,128)(2,1)}, u32[]{:S(2)}) copy-start(bf16[1,1024,1024]{2,1,0:T(8,128)(2,1)} %param.3) | copy-start | bytes 6291460
  9.2 27.2 %collective-permute-start.3 = (bf16[256,1024]{1,0:T(8,128)(2,1)S(1)}, bf16[256,1024]{1,0:T(8,128)(2,1)S(1)}, u32[]{:S(2)}, u32[]{:S(2)}) collective-permute-start(bf16[256,1024]{1,0:T(8,128)(2,1)S(1)} %get-tuple-element.41), channel_id=1, source_target_pairs={{0,16},{8,24},{16,0},{24,8},{1,17},{9,25},{17,1},{25,9},{2,18},{10... | collective-permute-start | bytes 1572872 | tf_op jit(solution)/shard_map/ppermute | solution.py:13
  36.4 13.1 %collective-permute-start.4 = (bf16[256,1024]{1,0:T(8,128)(2,1)S(1)}, bf16[256,1024]{1,0:T(8,128)(2,1)S(1)}, u32[]{:S(2)}, u32[]{:S(2)}) collective-permute-start(bf16[256,1024]{1,0:T(8,128)(2,1)S(1)} %collective-permute-done.3), channel_id=1, source_target_pairs={{0,1},{1,0},{2,3},{3,2},{4,5},{5,4},{6,7},{7,6},{8,9},{9,8},{10,11... | collective-permute-start | bytes 1572872 | tf_op jit(solution)/shard_map/ppermute | solution.py:13
  38.0 24.7 %collective-permute-start.2 = (bf16[256,1024]{1,0:T(8,128)(2,1)S(1)}, bf16[256,1024]{1,0:T(8,128)(2,1)S(1)}, u32[]{:S(2)}, u32[]{:S(2)}) collective-permute-start(bf16[256,1024]{1,0:T(8,128)(2,1)S(1)} %get-tuple-element.42), channel_id=1, source_target_pairs={{0,16},{8,24},{16,0},{24,8},{1,17},{9,25},{17,1},{25,9},{2,18},{10... | collective-permute-start | bytes 1572872 | tf_op jit(solution)/shard_map/ppermute | solution.py:13
  65.3 2.7 copy-start.7
  65.3 63.1 %all-gather.5.cloned.1.call-start = ((), (), s32[]{:S(2)}) async-start(), calls=%async_computation.5 | async-start | bytes 1310720 | tf_op jit(solution)/shard_map/all_gather | solution.py:123
  65.4 12.1 %collective-permute-start.5 = (bf16[256,1024]{1,0:T(8,128)(2,1)S(1)}, bf16[256,1024]{1,0:T(8,128)(2,1)}, u32[]{:S(2)}, u32[]{:S(2)}) collective-permute-start(bf16[256,1024]{1,0:T(8,128)(2,1)S(1)} %collective-permute-done.2), channel_id=1, source_target_pairs={{0,1},{1,0},{2,3},{3,2},{4,5},{5,4},{6,7},{7,6},{8,9},{9,8},{10,11... | collective-permute-start | bytes 1572872 | tf_op jit(solution)/shard_map/ppermute | solution.py:13
  66.2 24.2 %collective-permute-start.1 = (bf16[256,1024]{1,0:T(8,128)(2,1)}, bf16[256,1024]{1,0:T(8,128)(2,1)S(1)}, u32[]{:S(2)}, u32[]{:S(2)}) collective-permute-start(bf16[256,1024]{1,0:T(8,128)(2,1)} %get-tuple-element.43), channel_id=1, source_target_pairs={{0,16},{8,24},{16,0},{24,8},{1,17},{9,25},{17,1},{25,9},{2,18},{10... | collective-permute-start | bytes 1572872 | tf_op jit(solution)/shard_map/ppermute | solution.py:13
  90.4 10.6 %copy-start.6 = (bf16[256,1024]{1,0:T(8,128)(2,1)}, bf16[256,1024]{1,0:T(8,128)(2,1)S(1)}, u32[]{:S(2)}) copy-start(bf16[256,1024]{1,0:T(8,128)(2,1)S(1)} %collective-permute-done.1) | copy-start | bytes 1572868
  96.6 51.2 %reduce-scatter.7.cloned.1.call-start = ((), (), s32[]{:S(2)}) async-start(), calls=%async_computation.6 | async-start | bytes 2621440 | tf_op jit(solution)/shard_map/reduce_scatter | solution.py:114
  100.9 68.2 %all-gather.7.cloned.1.call-start = ((), (), s32[]{:S(2)}) async-start(), calls=%async_computation.7 | async-start | bytes 1310720 | tf_op jit(solution)/shard_map/all_gather | solution.py:123
  101.0 13.8 %collective-permute-start.6 = (bf16[256,1024]{1,0:T(8,128)(2,1)S(1)}, bf16[256,1024]{1,0:T(8,128)(2,1)S(1)}, u32[]{:S(2)}, u32[]{:S(2)}) collective-permute-start(bf16[256,1024]{1,0:T(8,128)(2,1)S(1)} %collective-permute-done.1), channel_id=1, source_target_pairs={{0,1},{1,0},{2,3},{3,2},{4,5},{5,4},{6,7},{7,6},{8,9},{9,8},{10,11... | collective-permute-start | bytes 1572872 | tf_op jit(solution)/shard_map/ppermute | solution.py:13
  102.5 25.8 %collective-permute-start = (bf16[256,1024]{1,0:T(8,128)(2,1)}, bf16[256,1024]{1,0:T(8,128)(2,1)}, u32[]{:S(2)}, u32[]{:S(2)}) collective-permute-start(bf16[256,1024]{1,0:T(8,128)(2,1)} %get-tuple-element.44), channel_id=1, source_target_pairs={{0,16},{8,24},{16,0},{24,8},{1,17},{9,25},{17,1},{25,9},{2,18},{10... | collective-permute-start | bytes 1572872 | tf_op jit(solution)/shard_map/ppermute | solution.py:13
  149.7 50.9 %reduce-scatter.9.cloned.1.call-start = ((), (), s32[]{:S(2)}) async-start(), calls=%async_computation.8 | async-start | bytes 2621440 | tf_op jit(solution)/shard_map/reduce_scatter | solution.py:114
  154.0 65.5 %all-gather.9.cloned.1.call-start = ((), (), s32[]{:S(2)}) async-start(), calls=%async_computation.9 | async-start | bytes 1310720 | tf_op jit(solution)/shard_map/all_gather | solution.py:123
  154.0 13.9 %collective-permute-start.7 = (bf16[256,1024]{1,0:T(8,128)(2,1)}, bf16[256,1024]{1,0:T(8,128)(2,1)S(1)}, u32[]{:S(2)}, u32[]{:S(2)}) collective-permute-start(bf16[256,1024]{1,0:T(8,128)(2,1)} %collective-permute-done), channel_id=1, source_target_pairs={{0,1},{1,0},{2,3},{3,2},{4,5},{5,4},{6,7},{7,6},{8,9},{9,8},{10,11... | collective-permute-start | bytes 1572872 | tf_op jit(solution)/shard_map/ppermute | solution.py:13
  169.1 33.5 %copy-start.4 = (bf16[512,1024]{1,0:T(8,128)(2,1)}, bf16[512,1024]{1,0:T(8,128)(2,1)S(1)}, u32[]{:S(2)}) copy-start(bf16[512,1024]{1,0:T(8,128)(2,1)S(1)} %pad_maximum_fusion.3) | copy-start | bytes 3145732
  202.5 51.2 %reduce-scatter.11.cloned.1.call-start = ((), (), s32[]{:S(2)}) async-start(), calls=%async_computation.10 | async-start | bytes 2621440 | tf_op jit(solution)/shard_map/reduce_scatter | solution.py:114
  206.8 1.2 copy-start.3
  206.8 65.8 %all-gather.11.cloned.1.call-start = ((), (), s32[]{:S(2)}) async-start(), calls=%async_computation.11 | async-start | bytes 1310720 | tf_op jit(solution)/shard_map/all_gather | solution.py:123
  208.0 2.3 copy-start
  219.5 36.1 %copy-start.1 = (bf16[1024,512]{0,1:T(8,128)(2,1)S(1)}, bf16[1024,512]{0,1:T(8,128)(2,1)}, u32[]{:S(2)}) copy-start(bf16[1024,512]{0,1:T(8,128)(2,1)} %all-gather.9.cloned.1.call-done) | copy-start | bytes 3145732
  255.6 17.0 %copy-start.5 = (bf16[512,1024]{1,0:T(8,128)(2,1)S(1)}, bf16[512,1024]{1,0:T(8,128)(2,1)}, u32[]{:S(2)}) copy-start(bf16[512,1024]{1,0:T(8,128)(2,1)} %copy-done.4) | copy-start | bytes 3145732
  (1 other events, 0.9 us)
Sparse Core Ops, SparseCore 0:
  65.4 29.2 reduce-scatter.4
  96.8 16.8 all-gather.4
  116.3 31.4 reduce-scatter.6
  149.8 16.8 all-gather.6
  169.1 31.4 reduce-scatter.8
  202.6 16.8 all-gather.8
  222.2 31.4 reduce-scatter.10
  255.7 16.8 all-gather.10
where the time goes:
time: 285 us
  waiting for transfers between devices  206 us (72%)
  matrix products  31.7 us (11%)
  between operations  14.8 us (5%)
  other arithmetic  14 us (5%)
  starting transfers between devices  12.4 us (4%)
  local copies, waits for them, and re-layouts  5.35 us (2%)
    ppermute x8, waiting for transfers between devices, shifted_2(): lax.ppermute(value, axis, [(i, (i + by) % count) for i in range(count)])  99 us
    reduce_scatter x4, waiting for transfers between devices, reduce(): lax.psum_scatter(partial, 'aux', scatter_dimension=0, tiled=True)  89.4 us
    all_gather x4, waiting for transfers between devices, amplitudes_of(): return lax.all_gather(amplitudes, 'aux', axis=0, tiled=True)  17.8 us
    dot_general x4, matrix products, paired_plan(): term = jnp.dot(gathered[c], blocks[c], preferred_element_type=jnp.float32)  16.5 us
    dot_general x4, matrix products, reduce(): jnp.einsum('aq,bq->ab', own, block, preferred_element_type=jnp.float32)  15.2 us
    ppermute x8, starting transfers between devices, shifted_2(): lax.ppermute(value, axis, [(i, (i + by) % count) for i in range(count)])  11.9 us
    convert_element_type x4, other arithmetic, amplitudes_of(): (summed / (pair_level - row_level[:, None] - col_level[None, :])).astype(...  7.58 us
  transfers between devices with their start and end apart: 16, of which 14 were waited for; matrix products, arithmetic and copies ran while one was open for 11% of the time, Pallas kernels for 0%

commit v1 on v0

--- a/solution.py
+++ b/solution.py
@@ -1,3 +1,4 @@
+import functools
 import jax
 import jax.numpy as jnp
 from jax import lax
@@ -6,6 +7,37 @@
 CHUNKS = 4
 AUX_BY_PERMUTE = False
 Z_GATED = False
+
+
+def settle_wires_all(raw, peer_axis):
+    z, moved, p_next = (lax.axis_size(peer_axis), lax.axis_index(peer_axis), raw.shape[0])
+    table = []
+    for dd, src_i in enumerate(raw.shape):
+        table.append(src_i * z if dd == 0 else src_i)
+    earlier = frame_out = raw
+    met_up = lax.dynamic_update_slice_in_dim(
+        jnp.zeros(table, raw.dtype), raw, moved * p_next, axis=0
+    )
+    for nth in range(1, z // 2 + 1):
+        buffer = []
+        for dd in range(z):
+            buffer.append((dd, (dd + 1) % z))
+        earlier = lax.ppermute(earlier, axis_name=peer_axis, perm=buffer)
+        met_up = lax.dynamic_update_slice_in_dim(
+            met_up, earlier, (moved - nth) % z * p_next, axis=0
+        )
+        if 2 * nth < z:
+            slots = []
+            for dd in range(z):
+                slots.append((dd, (dd - 1) % z))
+            frame_out = lax.ppermute(frame_out, axis_name=peer_axis, perm=slots)
+            met_up = lax.dynamic_update_slice_in_dim(
+                met_up, frame_out, (moved + nth) % z * p_next, axis=0
+            )
+    return met_up
+
+
+_fit_node = functools.partial(settle_wires_all, peer_axis="aux")
 
 
 def shifted_2(value, axis, by):
@@ -120,7 +152,7 @@
         )
         if AUX_BY_PERMUTE:
             return aux_all_gather(amplitudes)
-        return lax.all_gather(amplitudes, "aux", axis=0, tiled=True)
+        return _fit_node(amplitudes)
 
     arrived = [None] * CHUNKS
     blocks = [None] * CHUNKS

time: 285 us -> 227 us (0.80)
  waiting for transfers between devices: 206 us -> 151 us
  matrix products: 31.7 us -> 22 us
  starting transfers between devices: 12.4 us -> 19.2 us
    reduce_scatter x4, waiting for transfers between devices: 89.4 us -> 34.2 us  [reduce(): lax.psum_scatter(partial, 'aux', scatter_dimension=0, tiled=True)]
    ppermute x0 -> x12, waiting for transfers between devices: none -> 25.4 us  [the longest x8 25.3 us: settle_wires_all(): earlier = lax.ppermute(earlier, axis_name=peer_axis, perm=buffer)]
    all_gather x4 -> x0, waiting for transfers between devices: 17.8 us -> none  [amplitudes_of(): return lax.all_gather(amplitudes, 'aux', axis=0, tiled=True)]
    dot_general x4, matrix products: 16.5 us -> 8.4 us  [paired_plan(): term = jnp.dot(gathered[c], blocks[c], preferred_element_type=jnp.float32)]
    convert_element_type x4 -> x0, other arithmetic: 7.58 us -> none  [amplitudes_of(): (summed / (pair_level - row_level[:, None] - col_level[None, :])).astype(...]
    ppermute x8, waiting for transfers between devices: 99 us -> 91.7 us  [shifted_2(): lax.ppermute(value, axis, [(i, (i + by) % count) for i in range(count)])]
    ppermute x0 -> x12, starting transfers between devices: none -> 7.26 us  [the longest x4 6.97 us: settle_wires_all(): frame_out = lax.ppermute(frame_out, axis_name=peer_axis, perm=slots)]
    dynamic_update_slice x0 -> x4, other arithmetic: none -> 3.71 us  [settle_wires_all(): lax.dynamic_update_slice_in_dim(jnp.zeros(table, raw.dtype), raw, moved *...]
  transfers between devices with their start and end apart: 16 -> 24, of which waited for: 14 -> 18; matrix products, arithmetic and copies ran while one was open for 11% -> 8% of each run, Pallas kernels for 0% -> 0%
where the time goes in v1:
time: 227 us; the launch traced here: 226 us
  waiting for transfers between devices  151 us (67%)
  matrix products  22 us (10%)
  starting transfers between devices  19.2 us (8%)
  between operations  14.9 us (7%)
  other arithmetic  14.3 us (6%)
  local copies, waits for them, and re-layouts  4.72 us (2%)
    ppermute x8, waiting for transfers between devices, shifted_2(): lax.ppermute(value, axis, [(i, (i + by) % count) for i in range(count)])  91.7 us
    reduce_scatter x4, waiting for transfers between devices, reduce(): lax.psum_scatter(partial, 'aux', scatter_dimension=0, tiled=True)  34.2 us
    ppermute x8, waiting for transfers between devices, settle_wires_all(): earlier = lax.ppermute(earlier, axis_name=peer_axis, perm=buffer)  25.3 us
    dot_general x4, matrix products, reduce(): jnp.einsum('aq,bq->ab', own, block, preferred_element_type=jnp.float32)  13.6 us
    ppermute x8, starting transfers between devices, shifted_2(): lax.ppermute(value, axis, [(i, (i + by) % count) for i in range(count)])  11.8 us
    dot_general x4, matrix products, paired_plan(): term = jnp.dot(gathered[c], blocks[c], preferred_element_type=jnp.float32)  8.4 us
    ppermute x4, starting transfers between devices, settle_wires_all(): frame_out = lax.ppermute(frame_out, axis_name=peer_axis, perm=slots)  6.97 us
  transfers between devices with their start and end apart: 24, of which 18 were waited for; matrix products, arithmetic and copies ran while one was open for 8% of the time, Pallas kernels for 0%

profile of v1, /device:TPU:0, one launch (start us, length us, event | category | flops | bytes accessed | tf_op | source)
XLA Modules:
  0.0 226.4 jit_solution(8714905639595808330)
XLA Ops:
  6.5 2.7 %slice_bitcast_fusion = (bf16[256,1024]{1,0:T(8,128)(2,1)S(1)}, bf16[256,1024]{1,0:T(8,128)(2,1)S(1)}, bf16[256,1024]{1,0:T(8,128)(2,1)}, bf16[256,1024]{1,0:T(8,128)(2,1)}) fusion(bf16[1,1024,1024]{2,1,0:T(8,128)(2,1)} %param.3), kind=kLoop, calls=%fused_computation.22 | loop fusion | bytes 4194304 | tf_op jit(solution)/shard_map/slice | solution.py:165
  9.2 4.0 %collective-permute-start.3 = (bf16[256,1024]{1,0:T(8,128)(2,1)S(1)}, bf16[256,1024]{1,0:T(8,128)(2,1)S(1)}, u32[]{:S(2)}, u32[]{:S(2)}) collective-permute-start(bf16[256,1024]{1,0:T(8,128)(2,1)S(1)} %get-tuple-element.49), channel_id=1, source_target_pairs={{0,16},{8,24},{16,0},{24,8},{1,17},{9,25},{17,1},{25,9},{2,18},{10... | collective-permute-start | bytes 1572872 | tf_op jit(solution)/shard_map/ppermute | solution.py:45
  13.3 23.2 %collective-permute-done.3 = bf16[256,1024]{1,0:T(8,128)(2,1)S(1)} collective-permute-done((bf16[256,1024]{1,0:T(8,128)(2,1)S(1)}, bf16[256,1024]{1,0:T(8,128)(2,1)S(1)}, u32[]{:S(2)}, u32[]{:S(2)}) %collective-permute-start.3) | collective-permute-done | bytes 524320 | tf_op jit(solution)/shard_map/ppermute | solution.py:45
  38.0 11.5 %collective-permute-done.4 = bf16[256,1024]{1,0:T(8,128)(2,1)S(1)} collective-permute-done((bf16[256,1024]{1,0:T(8,128)(2,1)S(1)}, bf16[256,1024]{1,0:T(8,128)(2,1)S(1)}, u32[]{:S(2)}, u32[]{:S(2)}) %collective-permute-start.4) | collective-permute-done | bytes 524320 | tf_op jit(solution)/shard_map/ppermute | solution.py:45
  49.6 13.2 %collective-permute-done.2 = bf16[256,1024]{1,0:T(8,128)(2,1)} collective-permute-done((bf16[256,1024]{1,0:T(8,128)(2,1)S(1)}, bf16[256,1024]{1,0:T(8,128)(2,1)}, u32[]{:S(2)}, u32[]{:S(2)}) %collective-permute-start.2) | collective-permute-done | bytes 524320 | tf_op jit(solution)/shard_map/ppermute | solution.py:45
  62.8 2.6 %fusion.9 = f32[1024,512]{0,1:T(8,128)} fusion(bf16[512,1024]{1,0:T(8,128)(2,1)S(1)} %pad_maximum_fusion, bf16[1,1024,1024]{2,1,0:T(8,128)(2,1)S(1)} %copy-done.7), kind=kOutput, calls=%fused_computation.10 | convolution fusion | flops 1073741824 | bytes 5242880 | tf_op jit(solution)/shard_map/aq,bq->ab/dot_general | solution.py:143
  66.3 11.3 %collective-permute-done.5 = bf16[256,1024]{1,0:T(8,128)(2,1)S(1)} collective-permute-done((bf16[256,1024]{1,0:T(8,128)(2,1)}, bf16[256,1024]{1,0:T(8,128)(2,1)S(1)}, u32[]{:S(2)}, u32[]{:S(2)}) %collective-permute-start.5) | collective-permute-done | bytes 524320 | tf_op jit(solution)/shard_map/ppermute | solution.py:45
  78.7 11.8 %collective-permute-done.1 = bf16[256,1024]{1,0:T(8,128)(2,1)} collective-permute-done((bf16[256,1024]{1,0:T(8,128)(2,1)}, bf16[256,1024]{1,0:T(8,128)(2,1)}, u32[]{:S(2)}, u32[]{:S(2)}) %collective-permute-start.1) | collective-permute-done | bytes 524320 | tf_op jit(solution)/shard_map/ppermute | solution.py:45
  90.6 4.3 %reduce-scatter.5.cloned.1.call-done = f32[256,512]{0,1:T(8,128)} async-done(((f32[1024,512]{0,1:T(8,128)}), f32[256,512]{0,1:T(8,128)}) %reduce-scatter.5.cloned.1.call-update) | async-done | bytes 524304 | tf_op jit(solution)/shard_map/reduce_scatter | solution.py:146
  94.9 2.6 %fusion.12 = f32[1024,512]{0,1:T(8,128)} fusion(bf16[512,1024]{1,0:T(8,128)(2,1)S(1)} %pad_maximum_fusion.1, bf16[1,1024,1024]{2,1,0:T(8,128)(2,1)S(1)} %copy-done.7), kind=kOutput, calls=%fused_computation.11 | convolution fusion | flops 1073741824 | bytes 5242880 | tf_op jit(solution)/shard_map/aq,bq->ab/dot_general | solution.py:143
  106.3 3.6 %collective-permute-done.7 = bf16[256,512]{0,1:T(8,128)(2,1)S(1)} collective-permute-done((bf16[256,512]{0,1:T(8,128)(2,1)S(1)}, bf16[256,512]{0,1:T(8,128)(2,1)S(1)}, u32[]{:S(2)}, u32[]{:S(2)}) %collective-permute-start.7) | collective-permute-done | bytes 262176 | tf_op jit(solution)/shard_map/ppermute | solution.py:25
  110.0 4.4 %collective-permute-done.6 = bf16[256,1024]{1,0:T(8,128)(2,1)} collective-permute-done((bf16[256,1024]{1,0:T(8,128)(2,1)}, bf16[256,1024]{1,0:T(8,128)(2,1)}, u32[]{:S(2)}, u32[]{:S(2)}) %collective-permute-start.6) | collective-permute-done | bytes 524320 | tf_op jit(solution)/shard_map/ppermute | solution.py:45
  115.8 13.4 %collective-permute-done = bf16[256,1024]{1,0:T(8,128)(2,1)} collective-permute-done((bf16[256,1024]{1,0:T(8,128)(2,1)}, bf16[256,1024]{1,0:T(8,128)(2,1)}, u32[]{:S(2)}, u32[]{:S(2)}) %collective-permute-start) | collective-permute-done | bytes 524320 | tf_op jit(solution)/shard_map/ppermute | solution.py:45
  129.1 4.2 %fusion.15 = f32[1024,512]{0,1:T(8,128)} fusion(bf16[512,1024]{1,0:T(8,128)(2,1)S(1)} %pad_maximum_fusion.2, bf16[1,1024,1024]{2,1,0:T(8,128)(2,1)} %param.3), kind=kOutput, calls=%fused_computation.12 | convolution fusion | flops 1073741824 | bytes 5242880 | tf_op jit(solution)/shard_map/aq,bq->ab/dot_general | solution.py:143
  137.9 3.6 %collective-permute-done.11 = bf16[256,512]{0,1:T(8,128)(2,1)S(1)} collective-permute-done((bf16[256,512]{0,1:T(8,128)(2,1)S(1)}, bf16[256,512]{0,1:T(8,128)(2,1)S(1)}, u32[]{:S(2)}, u32[]{:S(2)}) %collective-permute-start.11) | collective-permute-done | bytes 262176 | tf_op jit(solution)/shard_map/ppermute | solution.py:25
  141.6 4.5 %fusion.23 = f32[1024,1024]{1,0:T(8,128)} fusion(bf16[1024,512]{0,1:T(8,128)(2,1)S(1)} %constant_dynamic-update-slice_fusion.12, bf16[512,1024]{1,0:T(8,128)(2,1)} %copy-done.2), kind=kOutput, calls=%fused_computation.49 | convolution fusion | flops 1073741824 | bytes 6291456 | tf_op jit(solution)/shard_map/dot_general | solution.py:206
  147.4 3.0 %collective-permute-done.10 = bf16[256,1024]{1,0:T(8,128)(2,1)S(1)} collective-permute-done((bf16[256,1024]{1,0:T(8,128)(2,1)}, bf16[256,1024]{1,0:T(8,128)(2,1)S(1)}, u32[]{:S(2)}, u32[]{:S(2)}) %collective-permute-start.10) | collective-permute-done | bytes 524320 | tf_op jit(solution)/shard_map/ppermute | solution.py:45
  151.6 13.5 %reduce-scatter.9.cloned.1.call-done = f32[256,512]{0,1:T(8,128)} async-done(((f32[1024,512]{0,1:T(8,128)}), f32[256,512]{0,1:T(8,128)}) %reduce-scatter.9.cloned.1.call-update) | async-done | bytes 524304 | tf_op jit(solution)/shard_map/reduce_scatter | solution.py:146
  165.0 4.2 %fusion.18 = f32[1024,512]{0,1:T(8,128)} fusion(bf16[512,1024]{1,0:T(8,128)(2,1)S(1)} %pad_maximum_fusion.3, bf16[1,1024,1024]{2,1,0:T(8,128)(2,1)} %param.3), kind=kOutput, calls=%fused_computation.13 | convolution fusion | flops 1073741824 | bytes 5242880 | tf_op jit(solution)/shard_map/aq,bq->ab/dot_general | solution.py:143
  172.4 6.2 %collective-permute-done.14 = bf16[256,512]{0,1:T(8,128)(2,1)S(1)} collective-permute-done((bf16[256,512]{0,1:T(8,128)(2,1)S(1)}, bf16[256,512]{0,1:T(8,128)(2,1)S(1)}, u32[]{:S(2)}, u32[]{:S(2)}) %collective-permute-start.14) | collective-permute-done | bytes 262176 | tf_op jit(solution)/shard_map/ppermute | solution.py:25
  179.9 2.9 %add.178 = f32[1024,1024]{1,0:T(8,128)} add(f32[1024,1024]{1,0:T(8,128)S(1)} %copy-done, f32[1024,1024]{1,0:T(8,128)S(1)} %fusion.24) | non-fusion elementwise | flops 1048576 | bytes 12582912 | tf_op jit(solution)/shard_map/add | solution.py:207
  184.4 16.5 %reduce-scatter.11.cloned.1.call-done = f32[256,512]{0,1:T(8,128)} async-done(((f32[1024,512]{0,1:T(8,128)}), f32[256,512]{0,1:T(8,128)}) %reduce-scatter.11.cloned.1.call-update) | async-done | bytes 524304 | tf_op jit(solution)/shard_map/reduce_scatter | solution.py:146
  204.0 6.3 %collective-permute-done.17 = bf16[256,512]{0,1:T(8,128)(2,1)S(1)} collective-permute-done((bf16[256,512]{0,1:T(8,128)(2,1)S(1)}, bf16[256,512]{0,1:T(8,128)(2,1)S(1)}, u32[]{:S(2)}, u32[]{:S(2)}) %collective-permute-start.17) | collective-permute-done | bytes 262176 | tf_op jit(solution)/shard_map/ppermute | solution.py:25
  213.1 3.0 %collective-permute-done.19 = bf16[256,512]{0,1:T(8,128)(2,1)S(1)} collective-permute-done((bf16[256,512]{0,1:T(8,128)(2,1)S(1)}, bf16[256,512]{0,1:T(8,128)(2,1)S(1)}, u32[]{:S(2)}, u32[]{:S(2)}) %collective-permute-start.19) | collective-permute-done | bytes 262176 | tf_op jit(solution)/shard_map/ppermute | solution.py:25
  (92 shorter events, 35.2 us)
Async XLA Ops:
  6.5 88.3 %reduce-scatter.5.cloned.1.call-start = ((), (), s32[]{:S(2)}) async-start(), calls=%async_computation.4 | async-start | bytes 2621440 | tf_op jit(solution)/shard_map/reduce_scatter | solution.py:146
  9.2 27.2 %collective-permute-start.3 = (bf16[256,1024]{1,0:T(8,128)(2,1)S(1)}, bf16[256,1024]{1,0:T(8,128)(2,1)S(1)}, u32[]{:S(2)}, u32[]{:S(2)}) collective-permute-start(bf16[256,1024]{1,0:T(8,128)(2,1)S(1)} %get-tuple-element.49), channel_id=1, source_target_pairs={{0,16},{8,24},{16,0},{24,8},{1,17},{9,25},{17,1},{25,9},{2,18},{10... | collective-permute-start | bytes 1572872 | tf_op jit(solution)/shard_map/ppermute | solution.py:45
  36.4 13.1 %collective-permute-start.4 = (bf16[256,1024]{1,0:T(8,128)(2,1)S(1)}, bf16[256,1024]{1,0:T(8,128)(2,1)S(1)}, u32[]{:S(2)}, u32[]{:S(2)}) collective-permute-start(bf16[256,1024]{1,0:T(8,128)(2,1)S(1)} %collective-permute-done.3), channel_id=1, source_target_pairs={{0,1},{1,0},{2,3},{3,2},{4,5},{5,4},{6,7},{7,6},{8,9},{9,8},{10,11... | collective-permute-start | bytes 1572872 | tf_op jit(solution)/shard_map/ppermute | solution.py:45
  38.0 24.8 %collective-permute-start.2 = (bf16[256,1024]{1,0:T(8,128)(2,1)S(1)}, bf16[256,1024]{1,0:T(8,128)(2,1)}, u32[]{:S(2)}, u32[]{:S(2)}) collective-permute-start(bf16[256,1024]{1,0:T(8,128)(2,1)S(1)} %get-tuple-element.50), channel_id=1, source_target_pairs={{0,16},{8,24},{16,0},{24,8},{1,17},{9,25},{17,1},{25,9},{2,18},{10... | collective-permute-start | bytes 1572872 | tf_op jit(solution)/shard_map/ppermute | solution.py:45
  65.4 63.7 %reduce-scatter.7.cloned.1.call-start = ((), (), s32[]{:S(2)}) async-start(), calls=%async_computation.5 | async-start | bytes 2621440 | tf_op jit(solution)/shard_map/reduce_scatter | solution.py:146
  65.5 12.2 %collective-permute-start.5 = (bf16[256,1024]{1,0:T(8,128)(2,1)}, bf16[256,1024]{1,0:T(8,128)(2,1)S(1)}, u32[]{:S(2)}, u32[]{:S(2)}) collective-permute-start(bf16[256,1024]{1,0:T(8,128)(2,1)} %collective-permute-done.2), channel_id=1, source_target_pairs={{0,1},{1,0},{2,3},{3,2},{4,5},{5,4},{6,7},{7,6},{8,9},{9,8},{10,11... | collective-permute-start | bytes 1572872 | tf_op jit(solution)/shard_map/ppermute | solution.py:45
  66.3 24.3 %collective-permute-start.1 = (bf16[256,1024]{1,0:T(8,128)(2,1)}, bf16[256,1024]{1,0:T(8,128)(2,1)}, u32[]{:S(2)}, u32[]{:S(2)}) collective-permute-start(bf16[256,1024]{1,0:T(8,128)(2,1)} %get-tuple-element.51), channel_id=1, source_target_pairs={{0,16},{8,24},{16,0},{24,8},{1,17},{9,25},{17,1},{25,9},{2,18},{10... | collective-permute-start | bytes 1572872 | tf_op jit(solution)/shard_map/ppermute | solution.py:45
  97.5 67.5 %reduce-scatter.9.cloned.1.call-start = ((), (), s32[]{:S(2)}) async-start(), calls=%async_computation.6 | async-start | bytes 2621440 | tf_op jit(solution)/shard_map/reduce_scatter | solution.py:146
  100.3 14.0 %collective-permute-start.6 = (bf16[256,1024]{1,0:T(8,128)(2,1)}, bf16[256,1024]{1,0:T(8,128)(2,1)}, u32[]{:S(2)}, u32[]{:S(2)}) collective-permute-start(bf16[256,1024]{1,0:T(8,128)(2,1)} %collective-permute-done.1), channel_id=1, source_target_pairs={{0,1},{1,0},{2,3},{3,2},{4,5},{5,4},{6,7},{7,6},{8,9},{9,8},{10,11... | collective-permute-start | bytes 1572872 | tf_op jit(solution)/shard_map/ppermute | solution.py:45
  102.1 7.8 %collective-permute-start.7 = (bf16[256,512]{0,1:T(8,128)(2,1)S(1)}, bf16[256,512]{0,1:T(8,128)(2,1)S(1)}, u32[]{:S(2)}, u32[]{:S(2)}) collective-permute-start(bf16[256,512]{0,1:T(8,128)(2,1)S(1)} %get-tuple-element.48), channel_id=1, source_target_pairs={{0,2},{2,4},{4,6},{6,0},{1,3},{3,5},{5,7},{7,1},{8,10},{10,12},{12... | collective-permute-start | bytes 786440 | tf_op jit(solution)/shard_map/ppermute | solution.py:25
  102.1 7.8 %collective-permute-start.8 = (bf16[256,512]{0,1:T(8,128)(2,1)S(1)}, bf16[256,512]{0,1:T(8,128)(2,1)S(1)}, u32[]{:S(2)}, u32[]{:S(2)}) collective-permute-start(bf16[256,512]{0,1:T(8,128)(2,1)S(1)} %get-tuple-element.48), channel_id=1, source_target_pairs={{0,6},{2,0},{4,2},{6,4},{1,7},{3,1},{5,3},{7,5},{8,14},{10,8},{12,... | collective-permute-start | bytes 786440 | tf_op jit(solution)/shard_map/ppermute | solution.py:33
  103.9 25.2 %collective-permute-start = (bf16[256,1024]{1,0:T(8,128)(2,1)}, bf16[256,1024]{1,0:T(8,128)(2,1)}, u32[]{:S(2)}, u32[]{:S(2)}) collective-permute-start(bf16[256,1024]{1,0:T(8,128)(2,1)} %get-tuple-element.52), channel_id=1, source_target_pairs={{0,16},{8,24},{16,0},{24,8},{1,17},{9,25},{17,1},{25,9},{2,18},{10... | collective-permute-start | bytes 1572872 | tf_op jit(solution)/shard_map/ppermute | solution.py:45
  109.9 5.8 %collective-permute-start.9 = (bf16[256,512]{0,1:T(8,128)(2,1)S(1)}, bf16[256,512]{0,1:T(8,128)(2,1)S(1)}, u32[]{:S(2)}, u32[]{:S(2)}) collective-permute-start(bf16[256,512]{0,1:T(8,128)(2,1)S(1)} %collective-permute-done.7), channel_id=1, source_target_pairs={{0,2},{2,4},{4,6},{6,0},{1,3},{3,5},{5,7},{7,1},{8,10},{10,12},{12... | collective-permute-start | bytes 786440 | tf_op jit(solution)/shard_map/ppermute | solution.py:25
  133.3 67.6 %reduce-scatter.11.cloned.1.call-start = ((), (), s32[]{:S(2)}) async-start(), calls=%async_computation.7 | async-start | bytes 2621440 | tf_op jit(solution)/shard_map/reduce_scatter | solution.py:146
  134.7 6.8 %collective-permute-start.11 = (bf16[256,512]{0,1:T(8,128)(2,1)S(1)}, bf16[256,512]{0,1:T(8,128)(2,1)S(1)}, u32[]{:S(2)}, u32[]{:S(2)}) collective-permute-start(bf16[256,512]{0,1:T(8,128)(2,1)S(1)} %get-tuple-element.46), channel_id=1, source_target_pairs={{0,2},{2,4},{4,6},{6,0},{1,3},{3,5},{5,7},{7,1},{8,10},{10,12},{12... | collective-permute-start | bytes 786440 | tf_op jit(solution)/shard_map/ppermute | solution.py:25
  134.8 11.4 %collective-permute-start.12 = (bf16[256,512]{0,1:T(8,128)(2,1)S(1)}, bf16[256,512]{0,1:T(8,128)(2,1)S(1)}, u32[]{:S(2)}, u32[]{:S(2)}) collective-permute-start(bf16[256,512]{0,1:T(8,128)(2,1)S(1)} %get-tuple-element.46), channel_id=1, source_target_pairs={{0,6},{2,0},{4,2},{6,4},{1,7},{3,1},{5,3},{7,5},{8,14},{10,8},{12,... | collective-permute-start | bytes 786440 | tf_op jit(solution)/shard_map/ppermute | solution.py:33
  136.5 13.9 %collective-permute-start.10 = (bf16[256,1024]{1,0:T(8,128)(2,1)}, bf16[256,1024]{1,0:T(8,128)(2,1)S(1)}, u32[]{:S(2)}, u32[]{:S(2)}) collective-permute-start(bf16[256,1024]{1,0:T(8,128)(2,1)} %collective-permute-done), channel_id=1, source_target_pairs={{0,1},{1,0},{2,3},{3,2},{4,5},{5,4},{6,7},{7,6},{8,9},{9,8},{10,11... | collective-permute-start | bytes 1572872 | tf_op jit(solution)/shard_map/ppermute | solution.py:45
  141.6 5.8 %collective-permute-start.13 = (bf16[256,512]{0,1:T(8,128)(2,1)S(1)}, bf16[256,512]{0,1:T(8,128)(2,1)S(1)}, u32[]{:S(2)}, u32[]{:S(2)}) collective-permute-start(bf16[256,512]{0,1:T(8,128)(2,1)S(1)} %collective-permute-done.11), channel_id=1, source_target_pairs={{0,2},{2,4},{4,6},{6,0},{1,3},{3,5},{5,7},{7,1},{8,10},{10,12},{12... | collective-permute-start | bytes 786440 | tf_op jit(solution)/shard_map/ppermute | solution.py:25
  170.6 8.0 %collective-permute-start.14 = (bf16[256,512]{0,1:T(8,128)(2,1)S(1)}, bf16[256,512]{0,1:T(8,128)(2,1)S(1)}, u32[]{:S(2)}, u32[]{:S(2)}) collective-permute-start(bf16[256,512]{0,1:T(8,128)(2,1)S(1)} %get-tuple-element.44), channel_id=1, source_target_pairs={{0,2},{2,4},{4,6},{6,0},{1,3},{3,5},{5,7},{7,1},{8,10},{10,12},{12... | collective-permute-start | bytes 786440 | tf_op jit(solution)/shard_map/ppermute | solution.py:25
  170.7 12.2 %collective-permute-start.15 = (bf16[256,512]{0,1:T(8,128)(2,1)S(1)}, bf16[256,512]{0,1:T(8,128)(2,1)S(1)}, u32[]{:S(2)}, u32[]{:S(2)}) collective-permute-start(bf16[256,512]{0,1:T(8,128)(2,1)S(1)} %get-tuple-element.44), channel_id=1, source_target_pairs={{0,6},{2,0},{4,2},{6,4},{1,7},{3,1},{5,3},{7,5},{8,14},{10,8},{12,... | collective-permute-start | bytes 786440 | tf_op jit(solution)/shard_map/ppermute | solution.py:33
  178.6 5.8 %collective-permute-start.16 = (bf16[256,512]{0,1:T(8,128)(2,1)S(1)}, bf16[256,512]{0,1:T(8,128)(2,1)S(1)}, u32[]{:S(2)}, u32[]{:S(2)}) collective-permute-start(bf16[256,512]{0,1:T(8,128)(2,1)S(1)} %collective-permute-done.14), channel_id=1, source_target_pairs={{0,2},{2,4},{4,6},{6,0},{1,3},{3,5},{5,7},{7,1},{8,10},{10,12},{12... | collective-permute-start | bytes 786440 | tf_op jit(solution)/shard_map/ppermute | solution.py:25
  202.2 8.1 %collective-permute-start.17 = (bf16[256,512]{0,1:T(8,128)(2,1)S(1)}, bf16[256,512]{0,1:T(8,128)(2,1)S(1)}, u32[]{:S(2)}, u32[]{:S(2)}) collective-permute-start(bf16[256,512]{0,1:T(8,128)(2,1)S(1)} %get-tuple-element.42), channel_id=1, source_target_pairs={{0,2},{2,4},{4,6},{6,0},{1,3},{3,5},{5,7},{7,1},{8,10},{10,12},{12... | collective-permute-start | bytes 786440 | tf_op jit(solution)/shard_map/ppermute | solution.py:25
  202.3 10.7 %collective-permute-start.18 = (bf16[256,512]{0,1:T(8,128)(2,1)S(1)}, bf16[256,512]{0,1:T(8,128)(2,1)S(1)}, u32[]{:S(2)}, u32[]{:S(2)}) collective-permute-start(bf16[256,512]{0,1:T(8,128)(2,1)S(1)} %get-tuple-element.42), channel_id=1, source_target_pairs={{0,6},{2,0},{4,2},{6,4},{1,7},{3,1},{5,3},{7,5},{8,14},{10,8},{12,... | collective-permute-start | bytes 786440 | tf_op jit(solution)/shard_map/ppermute | solution.py:33
  210.3 5.8 %collective-permute-start.19 = (bf16[256,512]{0,1:T(8,128)(2,1)S(1)}, bf16[256,512]{0,1:T(8,128)(2,1)S(1)}, u32[]{:S(2)}, u32[]{:S(2)}) collective-permute-start(bf16[256,512]{0,1:T(8,128)(2,1)S(1)} %collective-permute-done.17), channel_id=1, source_target_pairs={{0,2},{2,4},{4,6},{6,0},{1,3},{3,5},{5,7},{7,1},{8,10},{10,12},{12... | collective-permute-start | bytes 786440 | tf_op jit(solution)/shard_map/ppermute | solution.py:25
  (11 other events, 163.9 us)
Sparse Core Ops, SparseCore 0:
  65.5 29.2 reduce-scatter.4
  97.6 31.3 reduce-scatter.6
  133.5 31.5 reduce-scatter.8
  169.4 31.4 reduce-scatter.10
